TPU v7x, 128 devices: a whole 4x4x4 slice. The times are simulated.
128 devices in a mesh: row: 32 (over y, z_lo, x), col: 4 (over z_hi, core).
Axes of the slice: x: 4, y: 4, z: 4 (z_hi: 2, z_lo: 2; z = z_hi * 2 + z_lo), core: 2. Of those that a mesh axis runs over, the one named last changes fastest.
Arguments:
- ratings: bfloat16 [4, 262144, 512], P(None, ('row', 'col'))
- tile_mask: int32 [4, 2048, 4], P(None, ('row', 'col')), may hold values from 0 to 1, as said below
- tile_counts: int32 [128], replicated, may hold values from 1 to 16, as said below
- users: float32 [131072, 128], P(('row', 'col')), may hold values from -2 to 2
- user_accum: float32 [131072, 128], P(('row', 'col')), may hold values from 0.05 to 0.5
- items: float32 [65536, 128], P(('row', 'col')), may hold values from -2 to 2
- item_accum: float32 [65536, 128], P(('row', 'col')), may hold values from 0.05 to 0.5
Outputs:
- users_out: float32 [131072, 128], P(('row', 'col'))
- user_accum_out: float32 [131072, 128], P(('row', 'col'))
- items_out: float32 [65536, 128], P(('row', 'col'))
- item_accum_out: float32 [65536, 128], P(('row', 'col'))
- losses: float32 [4], replicated
Inputs may be any that keep to these rules, and one draw needn't show every extreme that they name: Each group of 4 positions has tile_counts summing to 32, and exactly one position of each group, not always the same, owns 2 * 8 tiles. `tile_mask`: in each stratum, the first slot's first item tile of every position is 1.
All inputs are finite; a program needn't handle non-finite values.
Results may differ from a plain program's by a relative error of at most 0.0025.
Values sent between devices are 32-bit elements; how exact they have to be, the bound alone decides.
No kernel may reach another device: no remote copies, remote signals or barrier semaphores. Data moves between devices by JAX's collectives and lax.ppermute only.
A program may use at most 64 MiB of HBM per device.

v0:
```python
import jax
import jax.numpy as jnp
from jax import lax
from jax.sharding import PartitionSpec as P

TILE = 128
UT = 8
STEPS = 3
ridge_weight = 0.02
step_rate = 0.05


def passed_along(value, axis, steps):
    count = lax.axis_size(axis)
    pairs = [(source, (source + steps) % count) for source in range(count)]
    return lax.ppermute(value, axis, pairs)


def update(user_fac, user_acc, item_fac, item_acc, rating_block, live_tiles):
    tile_size = user_fac.shape[0] // live_tiles.shape[0]
    user_half = user_fac.astype(jnp.bfloat16)
    item_half = item_fac.astype(jnp.bfloat16)
    predicted = lax.dot_general(
        user_half, item_half, (((1,), (1,)), ((), ())), preferred_element_type=jnp.float32
    )
    residue = predicted - rating_block.astype(jnp.float32)
    masked = (
        residue.reshape(live_tiles.shape[0], tile_size, live_tiles.shape[1], tile_size)
        * live_tiles[:, None, :, None]
    ).reshape(residue.shape)
    sq_error = jnp.sum(masked * residue)
    err_half = masked.astype(jnp.bfloat16)
    grad_user = (
        jnp.dot(err_half, item_half, preferred_element_type=jnp.float32)
        * float(item_fac.shape[0]) ** (-0.5)
        + ridge_weight * user_fac
    )
    grad_item = (
        lax.dot_general(
            err_half, user_half, (((0,), (0,)), ((), ())), preferred_element_type=jnp.float32
        )
        * float(UT * TILE) ** (-0.5)
        + ridge_weight * item_fac
    )
    user_acc = user_acc + grad_user * grad_user
    item_acc = item_acc + grad_item * grad_item
    user_fac = user_fac - step_rate * grad_user * lax.rsqrt(user_acc)
    item_fac = item_fac - step_rate * grad_item * lax.rsqrt(item_acc)
    return (user_fac, user_acc, item_fac, item_acc, sq_error)


def on_device(ratings, tile_mask, tile_counts, users, user_accum, items, item_accum):
    strata_count = ratings.shape[0]
    slot_count = tile_mask.shape[1]
    tile_size = ratings.shape[1] // slot_count
    group_size = lax.axis_size("col")
    member = lax.axis_index("col")
    arrived_rows = users.shape[0]
    group_counts = lax.dynamic_slice_in_dim(
        tile_counts, lax.axis_index("row") * group_size, group_size
    )
    ranks = jnp.arange(group_size, dtype=jnp.int32)
    start_tile = jnp.sum(jnp.where(ranks < member, group_counts, 0))
    own_count = jnp.sum(jnp.where(ranks == member, group_counts, 0))
    valid = (jnp.arange(slot_count, dtype=jnp.int32) < own_count).astype(jnp.float32)
    whole_fac, whole_acc = (
        lax.all_gather(users, "col", axis=0, tiled=True),
        lax.all_gather(user_accum, "col", axis=0, tiled=True),
    )
    pad_rows = slot_count * tile_size
    ext_fac = jnp.concatenate([whole_fac, whole_fac[:pad_rows]], axis=0)
    ext_acc = jnp.concatenate([whole_acc, whole_acc[:pad_rows]], axis=0)
    user_fac = lax.dynamic_slice_in_dim(ext_fac, start_tile * tile_size, pad_rows, 0)
    user_acc = lax.dynamic_slice_in_dim(ext_acc, start_tile * tile_size, pad_rows, 0)
    held_pair = jnp.stack([items, item_accum])
    loss_list = []
    for stratum in range(strata_count):
        live_tiles = tile_mask[stratum].astype(jnp.float32) * valid[:, None]
        item_fac = held_pair[0]
        item_acc = held_pair[1]
        for inner in range(STEPS):
            user_fac, user_acc, item_fac, item_acc, sq_error = update(
                user_fac, user_acc, item_fac, item_acc, ratings[stratum], live_tiles
            )
            if inner == 0:
                observed = jnp.sum(live_tiles) * float(tile_size * tile_size)
                total_error, total_count = lax.psum((sq_error, observed), ("row", "col"))
                loss_list.append(total_error / total_count)
        held_pair = jnp.stack([item_fac, item_acc])
        if stratum + 1 < strata_count:
            held_pair = passed_along(held_pair, ("row", "col"), 1)
    losses = jnp.stack(loss_list)
    row_valid = jnp.repeat(valid, tile_size)[:, None] > 0.5
    kept_fac = jnp.where(row_valid, user_fac, 0.0)
    kept_acc = jnp.where(row_valid, user_acc, 0.0)
    frame_rows = group_size * arrived_rows + pad_rows
    frame_fac = lax.dynamic_update_slice_in_dim(
        jnp.zeros((frame_rows, kept_fac.shape[1]), jnp.float32), kept_fac, start_tile * tile_size, 0
    )
    frame_acc = lax.dynamic_update_slice_in_dim(
        jnp.zeros((frame_rows, kept_acc.shape[1]), jnp.float32), kept_acc, start_tile * tile_size, 0
    )
    users_new, accum_new = (
        lax.psum_scatter(
            frame_fac[: group_size * arrived_rows], "col", scatter_dimension=0, tiled=True
        ),
        lax.psum_scatter(
            frame_acc[: group_size * arrived_rows], "col", scatter_dimension=0, tiled=True
        ),
    )
    return (users_new, accum_new, held_pair[0], held_pair[1], losses)


def solution(mesh):
    return jax.shard_map(
        on_device,
        mesh=mesh,
        in_specs=(
            P(None, ("row", "col"), None),
            P(None, ("row", "col"), None),
            P(),
            P(("row", "col"), None),
            P(("row", "col"), None),
            P(("row", "col"), None),
            P(("row", "col"), None),
        ),
        out_specs=(
            P(("row", "col"), None),
            P(("row", "col"), None),
            P(("row", "col"), None),
            P(("row", "col"), None),
            P(),
        ),
        check_vma=False,
    )
```

profile of v0, /device:TPU:0, one launch (start us, length us, event | category | flops | bytes accessed | tf_op | source)
XLA Modules:
  0.0 266.9 jit_solution(3098577988542652203)
XLA Ops:
  7.2 0.7 all-gather.3.cloned.1.call-update
  7.9 0.7 all-gather.5.cloned.1.call-update
  8.7 1.4 fusion.113
  10.7 0.7 compare_convert_fusion
  11.4 1.4 fusion.118
  12.9 26.0 %all-gather.3.cloned.1.call-done = f32[4096,128]{1,0:T(8,128)} async-done(((f32[1024,128]{1,0:T(8,128)}), f32[4096,128]{1,0:T(8,128)}) %all-gather.3.cloned.1.call-update) | async-done | bytes 2097168 | tf_op jit(solution)/shard_map/all_gather | solution.py:67
  38.9 1.2 slice-done.7
  40.1 1.6 fusion.37
  41.8 0.6 mul.539
  42.7 4.7 %multiply_reduce_fusion.3 = (f32[]{:T(128)}, bf16[2048,512]{1,0:T(8,128)(2,1)S(1)}) fusion(f32[256,8,4,128]{3,2,1,0:T(4,128)S(1)} %bitcast.197, bf16[4,2048,512]{2,1,0:T(8,128)(2,1)} %param.7, f32[512,128]{1,0:T(8,128)S(1)} %copy-done.8, f32[2048,128]{1,0:T(8,128)S(1)} %fusion.37), kind=kOutput, calls=%fused_computation.35 | convolution fusion | flops 275054592 | bytes 9699332 | tf_op jit(solution)/shard_map/dot_general | solution.py:23
  47.4 1.5 multiply_subtract_fusion.19
  48.9 17.7 %all-gather.5.cloned.1.call-done = f32[4096,128]{1,0:T(8,128)} async-done(((f32[1024,128]{1,0:T(8,128)}), f32[4096,128]{1,0:T(8,128)}) %all-gather.5.cloned.1.call-update) | async-done | bytes 2097168 | tf_op jit(solution)/shard_map/all_gather | solution.py:68
  66.6 1.2 slice-done.6
  67.8 2.2 multiply_subtract_fusion.10
  70.3 2.4 fusion.1
  72.7 0.8 multiply_subtract_fusion.18
  73.5 1.7 multiply_subtract_fusion.9
  75.2 2.3 fusion.3
  77.5 0.8 subtract_bitcast_fusion.2
  78.3 0.8 pad_maximum_fusion
  79.4 2.3 multiply_subtract_fusion.8
  81.8 11.7 %collective-permute-done = f32[2,512,128]{2,1,0:T(8,128)} collective-permute-done((f32[2,512,128]{2,1,0:T(8,128)}, f32[2,512,128]{2,1,0:T(8,128)}, u32[]{:S(2)}, u32[]{:S(2)}) %collective-permute-start) | collective-permute-done | bytes 524320 | tf_op jit(solution)/shard_map/ppermute | solution.py:16
  93.5 0.6 mul.575
  94.1 3.7 %multiply_reduce_fusion.2 = (f32[]{:T(128)}, bf16[2048,512]{1,0:T(8,128)(2,1)S(1)}) fusion(f32[256,8,4,128]{3,2,1,0:T(4,128)S(1)} %bitcast.200, bf16[4,2048,512]{2,1,0:T(8,128)(2,1)} %param.7, f32[2,512,128]{2,1,0:T(8,128)} %collective-permute-done, f32[2048,128]{1,0:T(8,128)S(1)} %get-tuple-element.33), kind=kOutput, calls=%fused_computation.34 | convolution fusion | flops 274989056 | bytes 9568260 | tf_op jit(solution)/shard_map/dot_general | solution.py:23
  97.8 1.9 multiply_subtract_fusion.17
  99.8 1.7 multiply_subtract_fusion.7
  101.5 0.7 fusion.5
  102.2 1.7 multiply_subtract_fusion.6
  103.9 1.7 multiply_subtract_fusion.16
  105.6 0.7 fusion.7
  106.3 0.7 multiply_add_fusion.22
  107.1 1.0 subtract_bitcast_fusion.1
  108.1 0.8 pad_maximum_fusion.1
  109.1 0.7 broadcast_compare_fusion
  109.7 1.9 multiply_subtract_fusion.5
  111.7 11.7 %collective-permute-done.1 = f32[2,512,128]{2,1,0:T(8,128)} collective-permute-done((f32[2,512,128]{2,1,0:T(8,128)}, f32[2,512,128]{2,1,0:T(8,128)}, u32[]{:S(2)}, u32[]{:S(2)}) %collective-permute-start.1) | collective-permute-done | bytes 524320 | tf_op jit(solution)/shard_map/ppermute | solution.py:16
  123.3 0.6 mul.611
  124.0 3.7 %multiply_reduce_fusion.1 = (f32[]{:T(128)}, bf16[2048,512]{1,0:T(8,128)(2,1)S(1)}) fusion(f32[256,8,4,128]{3,2,1,0:T(4,128)S(1)} %bitcast.203, bf16[4,2048,512]{2,1,0:T(8,128)(2,1)} %param.7, f32[2,512,128]{2,1,0:T(8,128)} %collective-permute-done.1, f32[2048,128]{1,0:T(8,128)S(1)} %get-tuple-element.69), kind=kOutput, calls=%fused_computation.33 | convolution fusion | flops 274989056 | bytes 9568260 | tf_op jit(solution)/shard_map/dot_general | solution.py:23
  127.6 1.9 multiply_subtract_fusion.15
  129.6 1.7 multiply_subtract_fusion.4
  131.3 0.7 fusion.9
  132.2 1.7 multiply_subtract_fusion.3
  134.0 1.7 multiply_subtract_fusion.14
  135.7 0.7 fusion.11
  136.4 0.7 multiply_add_fusion.17
  137.2 1.0 subtract_bitcast_fusion
  138.2 0.8 pad_maximum_fusion.2
  139.2 2.3 multiply_subtract_fusion.2
  141.5 11.9 %collective-permute-done.2 = f32[2,512,128]{2,1,0:T(8,128)} collective-permute-done((f32[2,512,128]{2,1,0:T(8,128)}, f32[2,512,128]{2,1,0:T(8,128)}, u32[]{:S(2)}, u32[]{:S(2)}) %collective-permute-start.2) | collective-permute-done | bytes 524320 | tf_op jit(solution)/shard_map/ppermute | solution.py:16
  153.4 0.6 mul.647
  154.0 3.7 %multiply_reduce_fusion = (f32[]{:T(128)}, bf16[2048,512]{1,0:T(8,128)(2,1)S(1)}) fusion(f32[256,8,4,128]{3,2,1,0:T(4,128)S(1)} %bitcast.206, bf16[4,2048,512]{2,1,0:T(8,128)(2,1)} %param.7, f32[2,512,128]{2,1,0:T(8,128)} %collective-permute-done.2, f32[2048,128]{1,0:T(8,128)S(1)} %get-tuple-element.27), kind=kOutput, calls=%fused_computation.32 | convolution fusion | flops 274989056 | bytes 9568260 | tf_op jit(solution)/shard_map/dot_general | solution.py:23
  157.7 1.9 multiply_subtract_fusion.13
  159.7 1.8 multiply_subtract_fusion.1
  161.5 0.7 fusion.13
  162.2 0.7 multiply_subtract_fusion
  163.0 2.4 multiply_subtract_fusion.12
  165.4 0.7 fusion.15
  166.3 0.7 select_dynamic-update-slice_fusion.1
  167.0 1.6 copy-done.5
  169.2 1.4 slice.89
  170.8 3.1 %slice.88 = f32[4096,128]{1,0:T(8,128)} slice(f32[6144,128]{1,0:T(8,128)} %copy-done.5), slice={[0:4096], [0:128]} | slice | bytes 4194304 | tf_op jit(solution)/shard_map/slice | solution.py:105
  176.4 75.4 %all-reduce = (f32[]{:T(128)}, f32[]{:T(128)}, f32[]{:T(128)}, f32[]{:T(128)}, f32[]{:T(128)}, /*index=5*/f32[]{:T(128)}, f32[]{:T(128)}, f32[]{:T(128)}) all-reduce(f32[]{:T(128)} %get-tuple-element.45, f32[]{:T(128)S(6)} %mul.689, f32[]{:T(128)} %get-tuple-element.43, ...), channel_id=1, replica_groups=mesh['row'=32,'col'=4] {'row','col'}, use_global_device_ids=true, to_apply=%region_17.18 | all-reduce | flops 8 | bytes 64 | tf_op jit(solution)/shard_map/psum | solution.py:87
  257.1 0.6 pad_maximum_fusion.3
  257.7 2.6 multiply_subtract_fusion.11
  (61 shorter events, 2.5 us)
Async XLA Ops:
  7.2 31.8 %all-gather.3.cloned.1.call-start = ((), (), s32[]{:S(2)}) async-start(), calls=%async_computation.2 | async-start | bytes 2621440 | tf_op jit(solution)/shard_map/all_gather | solution.py:67
  7.9 58.7 %all-gather.5.cloned.1.call-start = ((), (), s32[]{:S(2)}) async-start(), calls=%async_computation.3 | async-start | bytes 2621440 | tf_op jit(solution)/shard_map/all_gather | solution.py:68
  8.6 251.7 %reduce-scatter.5.cloned.1.call-start = ((), (), s32[]{:S(2)}) async-start(), calls=%async_computation.5 | async-start | bytes 2621440 | tf_op jit(solution)/shard_map/reduce_scatter | solution.py:107
  38.9 1.2 slice-start.7
  41.8 1.0 copy-start.8
  42.4 5.0 %copy-start = (f32[16,128,4,128]{3,2,1,0:T(4,128)}, f32[16,128,4,128]{3,2,1,0:T(4,128)S(1)}, u32[]{:S(2)}) copy-start(f32[16,128,4,128]{3,2,1,0:T(4,128)S(1)} %mul.539) | copy-start | bytes 12582916
  42.7 4.7 %copy-start.10 = (f32[512,128]{1,0:T(8,128)S(1)}, f32[512,128]{1,0:T(8,128)}, u32[]{:S(2)}) copy-start(f32[512,128]{1,0:T(8,128)} %param.13) | copy-start | bytes 786436
  66.6 1.2 slice-start.6
  66.6 1.3 copy-start.9
  67.8 2.5 copy-start.1
  70.0 3.5 %copy-start.2 = (f32[2048,128]{1,0:T(8,128)}, f32[2048,128]{1,0:T(8,128)S(1)}, u32[]{:S(2)}) copy-start(f32[2048,128]{1,0:T(8,128)S(1)} %get-tuple-element.38) | copy-start | bytes 3145732
  70.3 2.4 copy-start.11
  70.3 2.4 copy-start.12
  73.5 4.0 %copy-start.6 = (f32[512,128]{1,0:T(8,128)}, f32[512,128]{1,0:T(8,128)S(1)}, u32[]{:S(2)}) copy-start(f32[512,128]{1,0:T(8,128)S(1)} %get-tuple-element.35) | copy-start | bytes 786436
  79.1 14.4 %collective-permute-start = (f32[2,512,128]{2,1,0:T(8,128)}, f32[2,512,128]{2,1,0:T(8,128)}, u32[]{:S(2)}, u32[]{:S(2)}) collective-permute-start(f32[2,512,128]{2,1,0:T(8,128)} %pad_maximum_fusion), channel_id=1, source_target_pairs={{0,1},{1,2},{2,3},{3,4},{4,5},{5,6},{6,7},{7,8},{8,9},{9,10},{10,1... | collective-permute-start | bytes 1572872 | tf_op jit(solution)/shard_map/ppermute | solution.py:16
  94.1 7.4 %slice-start = ((s8[8388608]{0:T(1024)(128)(4,1)}), s8[4194304]{0:T(1024)(128)(4,1)S(1)}, s32[]{:S(2)}) async-start(s8[8388608]{0:T(1024)(128)(4,1)} %bitcast.191), calls=%async_computation.6 | async-start | bytes 8388608
  97.8 3.6 %slice-start.1 = ((s8[8388608]{0:T(1024)(128)(4,1)}), s8[4194304]{0:T(1024)(128)(4,1)S(1)}, s32[]{:S(2)}) async-start(s8[8388608]{0:T(1024)(128)(4,1)} %bitcast.191), calls=%async_computation.7 | async-start | bytes 8388608
  109.0 14.4 %collective-permute-start.1 = (f32[2,512,128]{2,1,0:T(8,128)}, f32[2,512,128]{2,1,0:T(8,128)}, u32[]{:S(2)}, u32[]{:S(2)}) collective-permute-start(f32[2,512,128]{2,1,0:T(8,128)} %pad_maximum_fusion.1), channel_id=1, source_target_pairs={{0,1},{1,2},{2,3},{3,4},{4,5},{5,6},{6,7},{7,8},{8,9},{9,10},{10,1... | collective-permute-start | bytes 1572872 | tf_op jit(solution)/shard_map/ppermute | solution.py:16
  123.9 7.4 %slice-start.2 = ((s8[8388608]{0:T(1024)(128)(4,1)}), s8[4194304]{0:T(1024)(128)(4,1)S(1)}, s32[]{:S(2)}) async-start(s8[8388608]{0:T(1024)(128)(4,1)} %bitcast.193), calls=%async_computation.8 | async-start | bytes 8388608
  127.6 1.9 copy-start.3
  127.6 3.7 %slice-start.3 = ((s8[8388608]{0:T(1024)(128)(4,1)}), s8[4194304]{0:T(1024)(128)(4,1)S(1)}, s32[]{:S(2)}) async-start(s8[8388608]{0:T(1024)(128)(4,1)} %bitcast.193), calls=%async_computation.9 | async-start | bytes 8388608
  131.3 1.0 copy-start.4
  139.0 14.4 %collective-permute-start.2 = (f32[2,512,128]{2,1,0:T(8,128)}, f32[2,512,128]{2,1,0:T(8,128)}, u32[]{:S(2)}, u32[]{:S(2)}) collective-permute-start(f32[2,512,128]{2,1,0:T(8,128)} %pad_maximum_fusion.2), channel_id=1, source_target_pairs={{0,1},{1,2},{2,3},{3,4},{4,5},{5,6},{6,7},{7,8},{8,9},{9,10},{10,1... | collective-permute-start | bytes 1572872 | tf_op jit(solution)/shard_map/ppermute | solution.py:16
  154.0 7.5 %slice-start.4 = ((s8[8388608]{0:T(1024)(128)(4,1)}), s8[4194304]{0:T(1024)(128)(4,1)S(1)}, s32[]{:S(2)}) async-start(s8[8388608]{0:T(1024)(128)(4,1)} %bitcast.195), calls=%async_computation.10 | async-start | bytes 8388608
  157.7 3.7 %slice-start.5 = ((s8[8388608]{0:T(1024)(128)(4,1)}), s8[4194304]{0:T(1024)(128)(4,1)S(1)}, s32[]{:S(2)}) async-start(s8[8388608]{0:T(1024)(128)(4,1)} %bitcast.195), calls=%async_computation.11 | async-start | bytes 8388608
  159.7 3.3 %copy-start.7 = (f32[512,128]{1,0:T(8,128)}, f32[512,128]{1,0:T(8,128)S(1)}, u32[]{:S(2)}) copy-start(f32[512,128]{1,0:T(8,128)S(1)} %get-tuple-element.80) | copy-start | bytes 786436
  167.0 1.6 copy-start.5
  170.7 89.7 %reduce-scatter.3.cloned.1.call-start = ((), (), s32[]{:S(2)}) async-start(), calls=%async_computation.4 | async-start | bytes 2621440 | tf_op jit(solution)/shard_map/reduce_scatter | solution.py:104
Sparse Core Ops, SparseCore 0:
  9.6 29.2 all-gather.2
  40.6 25.9 all-gather.4
  170.8 31.6 reduce-scatter.4
  205.6 37.6 reduce-scatter.2
where the time goes:
time: 268 us; the launch traced here: 267 us
  waiting for transfers between devices  80.4 us (30%)
  blocking collectives  75.4 us (28%)
  matrix products  64 us (24%)
  between operations  22.7 us (8%)
  local copies, waits for them, and re-layouts  12.8 us (5%)
  other arithmetic  11.2 us (4%)
    psum x1, blocking collectives, on_device(): total_error, total_count = lax.psum((sq_error, observed), ('row', 'col'))  75.4 us
    ppermute x3, waiting for transfers between devices, passed_along(): return lax.ppermute(value, axis, pairs)  35.3 us
    all_gather x1, waiting for transfers between devices, on_device(): lax.all_gather(users, 'col', axis=0, tiled=True)  26 us
    dot_general x12, matrix products, update(): lax.dot_general(user_half, item_half, (((1,), (1,)), ((), ())), preferred...  24.8 us
    dot_general x12, matrix products, update(): jnp.dot(err_half, item_half, preferred_element_type=jnp.float32)  20.4 us
    dot_general x12, matrix products, update(): lax.dot_general(err_half, user_half, (((0,), (0,)), ((), ())), preferred_...  18.7 us
    all_gather x1, waiting for transfers between devices, on_device(): lax.all_gather(user_accum, 'col', axis=0, tiled=True)  17.7 us
  transfers between devices with their start and end apart: 7, of which 5 were waited for; matrix products, arithmetic and copies ran while one was open for 10% of the time, Pallas kernels for 0%

commit v1 on v0

--- a/solution.py
+++ b/solution.py
@@ -50,6 +50,19 @@
 
 
 def on_device(ratings, tile_mask, tile_counts, users, user_accum, items, item_accum):
+
+    def test_the_arrays(sheet, array_dim):
+        oldest = jnp.concatenate(
+            jax.lax.all_to_all(
+                jnp.stack(tuple((sheet for _ in range(jax.lax.axis_size("col")))), axis=0),
+                "col",
+                0,
+                0,
+            ),
+            axis=array_dim,
+        )
+        return oldest
+
     strata_count = ratings.shape[0]
     slot_count = tile_mask.shape[1]
     tile_size = ratings.shape[1] // slot_count
@@ -65,7 +78,7 @@
     valid = (jnp.arange(slot_count, dtype=jnp.int32) < own_count).astype(jnp.float32)
     whole_fac, whole_acc = (
         lax.all_gather(users, "col", axis=0, tiled=True),
-        lax.all_gather(user_accum, "col", axis=0, tiled=True),
+        test_the_arrays(user_accum, 0),
     )
     pad_rows = slot_count * tile_size
     ext_fac = jnp.concatenate([whole_fac, whole_fac[:pad_rows]], axis=0)

time: 268 us -> 258 us (0.963)
  waiting for transfers between devices: 80.4 us -> 71.9 us
  matrix products: 64 us -> 57.5 us
  starting transfers between devices: 0.39 us -> 5.48 us
    all_to_all x0 -> x1, waiting for transfers between devices: none -> 35.6 us  [test_the_arrays(): jax.lax.all_to_all(jnp.stack(tuple((sheet for _ in range(jax.lax.axis_siz...]
    all_gather x1, waiting for transfers between devices: 26 us -> 0.02 us  [on_device(): lax.all_gather(users, 'col', axis=0, tiled=True)]
    all_gather x1 -> x0, waiting for transfers between devices: 17.7 us -> none  [on_device(): lax.all_gather(user_accum, 'col', axis=0, tiled=True)]
    all_to_all x0 -> x1, starting transfers between devices: none -> 5.39 us  [test_the_arrays(): jax.lax.all_to_all(jnp.stack(tuple((sheet for _ in range(jax.lax.axis_siz...]
    dot_general x12, matrix products: 24.8 us -> 20.4 us  [update(): lax.dot_general(user_half, item_half, (((1,), (1,)), ((), ())), preferred...]
  transfers between devices with their start and end apart: 7 -> 7, of which waited for: 5 -> 4; matrix products, arithmetic and copies ran while one was open for 10% -> 7% of each run, Pallas kernels for 0% -> 0%
where the time goes in v1:
time: 258 us; the launch traced here: 257 us
  blocking collectives  75.8 us (29%)
  waiting for transfers between devices  71.9 us (28%)
  matrix products  57.5 us (22%)
  between operations  22.4 us (9%)
  local copies, waits for them, and re-layouts  14.4 us (6%)
  other arithmetic  9.85 us (4%)
  starting transfers between devices  5.48 us (2%)
    psum x1, blocking collectives, on_device(): total_error, total_count = lax.psum((sq_error, observed), ('row', 'col'))  75.8 us
    all_to_all x1, waiting for transfers between devices, test_the_arrays(): jax.lax.all_to_all(jnp.stack(tuple((sheet for _ in range(jax.lax.axis_siz...  35.6 us
    ppermute x3, waiting for transfers between devices, passed_along(): return lax.ppermute(value, axis, pairs)  35.6 us
    dot_general x12, matrix products, update(): lax.dot_general(user_half, item_half, (((1,), (1,)), ((), ())), preferred...  20.4 us
    dot_general x12, matrix products, update(): jnp.dot(err_half, item_half, preferred_element_type=jnp.float32)  19 us
    dot_general x12, matrix products, update(): lax.dot_general(err_half, user_half, (((0,), (0,)), ((), ())), preferred_...  18.1 us
    all_to_all x1, starting transfers between devices, test_the_arrays(): jax.lax.all_to_all(jnp.stack(tuple((sheet for _ in range(jax.lax.axis_siz...  5.39 us
  transfers between devices with their start and end apart: 7, of which 4 were waited for; matrix products, arithmetic and copies ran while one was open for 7% of the time, Pallas kernels for 0%

profile of v1, /device:TPU:0, one launch (start us, length us, event | category | flops | bytes accessed | tf_op | source)
XLA Modules:
  0.0 257.3 jit_solution(9082472004228521295)
XLA Ops:
  7.2 0.7 all-gather.2.cloned.1.call-update
  7.9 2.5 stack.49
  10.4 5.4 %all-to-all-start = ((f32[4,1024,128]{2,1,0:T(8,128)}), f32[4,1024,128]{2,1,0:T(8,128)S(1)}, u32[]{:S(2)}, u32[]{:S(2)}) async-start(f32[4,1024,128]{2,1,0:T(8,128)} %stack.49), calls=%async_computation | async-start | bytes 4194304 | tf_op jit(solution)/shard_map/all_to_all | solution.py:56
  15.8 0.7 fusion.113
  17.2 0.7 compare_convert_fusion
  17.8 0.7 fusion.118
  18.6 35.6 %all-to-all-done = f32[4,1024,128]{2,1,0:T(8,128)S(1)} async-done(((f32[4,1024,128]{2,1,0:T(8,128)}), f32[4,1024,128]{2,1,0:T(8,128)S(1)}, u32[]{:S(2)}, u32[]{:S(2)}) %all-to-all-start) | async-done | bytes 2097184 | tf_op jit(solution)/shard_map/all_to_all | solution.py:56
  54.3 1.2 slice-done.8
  55.5 1.6 fusion.37
  57.2 0.6 mul.539
  58.1 3.6 %multiply_reduce_fusion.3 = (f32[]{:T(128)}, bf16[2048,512]{1,0:T(8,128)(2,1)S(1)}) fusion(f32[256,8,4,128]{3,2,1,0:T(4,128)S(1)} %bitcast.201, bf16[4,2048,512]{2,1,0:T(8,128)(2,1)} %param.7, f32[512,128]{1,0:T(8,128)S(1)} %copy-done.5, f32[2048,128]{1,0:T(8,128)S(1)} %fusion.37), kind=kOutput, calls=%fused_computation.35 | convolution fusion | flops 275054592 | bytes 9699332 | tf_op jit(solution)/shard_map/dot_general | solution.py:23
  61.7 0.8 multiply_subtract_fusion.19
  62.5 0.8 multiply_subtract_fusion.10
  63.4 0.6 slice-done.1
  63.9 0.7 fusion.1
  64.6 0.8 multiply_subtract_fusion.18
  65.4 1.7 multiply_subtract_fusion.9
  67.1 0.7 fusion.3
  67.9 0.8 subtract_bitcast_fusion.2
  68.6 0.8 pad_maximum_fusion
  69.5 2.3 multiply_subtract_fusion.8
  71.8 12.0 %collective-permute-done = f32[2,512,128]{2,1,0:T(8,128)} collective-permute-done((f32[2,512,128]{2,1,0:T(8,128)}, f32[2,512,128]{2,1,0:T(8,128)}, u32[]{:S(2)}, u32[]{:S(2)}) %collective-permute-start) | collective-permute-done | bytes 524320 | tf_op jit(solution)/shard_map/ppermute | solution.py:16
  83.8 0.6 mul.575
  84.4 3.7 %multiply_reduce_fusion.2 = (f32[]{:T(128)}, bf16[2048,512]{1,0:T(8,128)(2,1)S(1)}) fusion(f32[256,8,4,128]{3,2,1,0:T(4,128)S(1)} %bitcast.204, bf16[4,2048,512]{2,1,0:T(8,128)(2,1)} %param.7, f32[2,512,128]{2,1,0:T(8,128)} %collective-permute-done, f32[2048,128]{1,0:T(8,128)S(1)} %get-tuple-element.33), kind=kOutput, calls=%fused_computation.34 | convolution fusion | flops 274989056 | bytes 9568260 | tf_op jit(solution)/shard_map/dot_general | solution.py:23
  88.1 1.9 multiply_subtract_fusion.17
  90.1 1.7 multiply_subtract_fusion.7
  91.8 0.7 fusion.5
  92.5 1.7 multiply_subtract_fusion.6
  94.2 1.7 multiply_subtract_fusion.16
  95.9 0.7 fusion.7
  96.6 0.7 multiply_add_fusion.22
  97.4 1.0 subtract_bitcast_fusion.1
  98.4 0.8 pad_maximum_fusion.1
  99.3 0.7 broadcast_compare_fusion
  100.0 1.9 multiply_subtract_fusion.5
  101.9 11.7 %collective-permute-done.1 = f32[2,512,128]{2,1,0:T(8,128)} collective-permute-done((f32[2,512,128]{2,1,0:T(8,128)}, f32[2,512,128]{2,1,0:T(8,128)}, u32[]{:S(2)}, u32[]{:S(2)}) %collective-permute-start.1) | collective-permute-done | bytes 524320 | tf_op jit(solution)/shard_map/ppermute | solution.py:16
  113.6 0.6 mul.611
  114.2 3.7 %multiply_reduce_fusion.1 = (f32[]{:T(128)}, bf16[2048,512]{1,0:T(8,128)(2,1)S(1)}) fusion(f32[256,8,4,128]{3,2,1,0:T(4,128)S(1)} %bitcast.207, bf16[4,2048,512]{2,1,0:T(8,128)(2,1)} %param.7, f32[2,512,128]{2,1,0:T(8,128)} %collective-permute-done.1, f32[2048,128]{1,0:T(8,128)S(1)} %get-tuple-element.69), kind=kOutput, calls=%fused_computation.33 | convolution fusion | flops 274989056 | bytes 9568260 | tf_op jit(solution)/shard_map/dot_general | solution.py:23
  117.9 1.9 multiply_subtract_fusion.15
  119.9 1.7 multiply_subtract_fusion.4
  121.6 0.7 fusion.9
  122.5 1.7 multiply_subtract_fusion.3
  124.3 1.7 multiply_subtract_fusion.14
  126.0 0.7 fusion.11
  126.7 0.7 multiply_add_fusion.17
  127.4 1.0 subtract_bitcast_fusion
  128.5 0.8 pad_maximum_fusion.2
  129.5 2.3 multiply_subtract_fusion.2
  131.8 11.9 %collective-permute-done.2 = f32[2,512,128]{2,1,0:T(8,128)} collective-permute-done((f32[2,512,128]{2,1,0:T(8,128)}, f32[2,512,128]{2,1,0:T(8,128)}, u32[]{:S(2)}, u32[]{:S(2)}) %collective-permute-start.2) | collective-permute-done | bytes 524320 | tf_op jit(solution)/shard_map/ppermute | solution.py:16
  143.7 0.6 mul.647
  144.3 3.7 %multiply_reduce_fusion = (f32[]{:T(128)}, bf16[2048,512]{1,0:T(8,128)(2,1)S(1)}) fusion(f32[256,8,4,128]{3,2,1,0:T(4,128)S(1)} %bitcast.210, bf16[4,2048,512]{2,1,0:T(8,128)(2,1)} %param.7, f32[2,512,128]{2,1,0:T(8,128)} %collective-permute-done.2, f32[2048,128]{1,0:T(8,128)S(1)} %get-tuple-element.27), kind=kOutput, calls=%fused_computation.32 | convolution fusion | flops 274989056 | bytes 9568260 | tf_op jit(solution)/shard_map/dot_general | solution.py:23
  148.0 1.9 multiply_subtract_fusion.13
  150.0 1.8 multiply_subtract_fusion.1
  151.8 0.7 fusion.13
  152.5 0.7 multiply_subtract_fusion
  153.2 2.4 multiply_subtract_fusion.12
  155.7 0.7 fusion.15
  156.6 0.7 select_dynamic-update-slice_fusion.1
  157.3 1.6 copy-done.3
  159.5 1.5 slice.93
  161.1 3.1 %slice.92 = f32[4096,128]{1,0:T(8,128)} slice(f32[6144,128]{1,0:T(8,128)} %copy-done.3), slice={[0:4096], [0:128]} | slice | bytes 4194304 | tf_op jit(solution)/shard_map/slice | solution.py:118
  166.7 75.8 %all-reduce = (f32[]{:T(128)}, f32[]{:T(128)}, f32[]{:T(128)}, f32[]{:T(128)}, f32[]{:T(128)}, /*index=5*/f32[]{:T(128)}, f32[]{:T(128)}, f32[]{:T(128)}) all-reduce(f32[]{:T(128)} %get-tuple-element.45, f32[]{:T(128)S(6)} %mul.689, f32[]{:T(128)} %get-tuple-element.43, ...), channel_id=1, replica_groups=mesh['row'=32,'col'=4] {'row','col'}, use_global_device_ids=true, to_apply=%region_17.18 | all-reduce | flops 8 | bytes 64 | tf_op jit(solution)/shard_map/psum | solution.py:100
  247.5 0.6 pad_maximum_fusion.3
  248.1 2.6 %multiply_subtract_fusion.11 = (f32[512,128]{1,0:T(8,128)}, f32[512,128]{1,0:T(8,128)}) fusion(f32[512,128]{1,0:T(8,128)S(1)} %get-tuple-element.81, f32[512,128]{1,0:T(8,128)} %get-tuple-element.82, f32[512,128]{1,0:T(8,128)} %copy-done.4, f32[2,512,128]{2,1,0:T(8,128)} %collective-permute-done.2, bf16[2048,512]{1,0:T(8,128)(2,1)S(1)} %fusion.15, ...), kind=kOutput, calls=%fused_computation.122 | convolution fusion | flops 269484032 | bytes 4718592 | tf_op jit(solution)/shard_map/dot_general | solution.py:39
  (57 shorter events, 2.0 us)
Async XLA Ops:
  7.2 47.1 %all-gather.2.cloned.1.call-start = ((), (), s32[]{:S(2)}) async-start(), calls=%async_computation.3 | async-start | bytes 2621440 | tf_op jit(solution)/shard_map/all_gather | solution.py:80
  10.4 5.4 %copy-start.8 = (s32[128]{0:T(128)S(1)}, s32[128]{0:T(128)}, u32[]{:S(2)}) copy-start(s32[128]{0:T(128)} %param.9) | copy-start | bytes 1540
  10.4 7.4 %copy-start.7 = (s32[4,16,4]{1,2,0:T(4,128)S(1)}, s32[4,16,4]{1,2,0:T(4,128)}, u32[]{:S(2)}) copy-start(s32[4,16,4]{1,2,0:T(4,128)} %param.8) | copy-start | bytes 3076
  10.4 43.8 %all-to-all-start = ((f32[4,1024,128]{2,1,0:T(8,128)}), f32[4,1024,128]{2,1,0:T(8,128)S(1)}, u32[]{:S(2)}, u32[]{:S(2)}) async-start(f32[4,1024,128]{2,1,0:T(8,128)} %stack.49), calls=%async_computation | async-start | bytes 4194304 | tf_op jit(solution)/shard_map/all_to_all | solution.py:56
  15.8 234.9 %reduce-scatter.5.cloned.1.call-start = ((), (), s32[]{:S(2)}) async-start(), calls=%async_computation.5 | async-start | bytes 2621440 | tf_op jit(solution)/shard_map/reduce_scatter | solution.py:120
  54.3 1.2 slice-start.8
  57.2 1.0 copy-start.5
  58.1 3.6 %copy-start.6 = (f32[512,128]{1,0:T(8,128)S(1)}, f32[512,128]{1,0:T(8,128)}, u32[]{:S(2)}) copy-start(f32[512,128]{1,0:T(8,128)} %param.13) | copy-start | bytes 786436
  58.1 5.2 %slice-start = ((s8[8388608]{0:T(1024)(128)(4,1)}), s8[4194304]{0:T(1024)(128)(4,1)S(1)}, s32[]{:S(2)}) async-start(s8[8388608]{0:T(1024)(128)(4,1)} %bitcast.193), calls=%async_computation.6 | async-start | bytes 8388608
  61.7 2.2 slice-start.1
  63.3 2.1 copy-start
  69.5 14.4 %collective-permute-start = (f32[2,512,128]{2,1,0:T(8,128)}, f32[2,512,128]{2,1,0:T(8,128)}, u32[]{:S(2)}, u32[]{:S(2)}) collective-permute-start(f32[2,512,128]{2,1,0:T(8,128)} %pad_maximum_fusion), channel_id=1, source_target_pairs={{0,1},{1,2},{2,3},{3,4},{4,5},{5,6},{6,7},{7,8},{8,9},{9,10},{10,1... | collective-permute-start | bytes 1572872 | tf_op jit(solution)/shard_map/ppermute | solution.py:16
  84.4 7.3 %slice-start.2 = ((s8[8388608]{0:T(1024)(128)(4,1)}), s8[4194304]{0:T(1024)(128)(4,1)S(1)}, s32[]{:S(2)}) async-start(s8[8388608]{0:T(1024)(128)(4,1)} %bitcast.195), calls=%async_computation.8 | async-start | bytes 8388608
  88.1 3.6 %slice-start.3 = ((s8[8388608]{0:T(1024)(128)(4,1)}), s8[4194304]{0:T(1024)(128)(4,1)S(1)}, s32[]{:S(2)}) async-start(s8[8388608]{0:T(1024)(128)(4,1)} %bitcast.195), calls=%async_computation.9 | async-start | bytes 8388608
  99.3 14.4 %collective-permute-start.1 = (f32[2,512,128]{2,1,0:T(8,128)}, f32[2,512,128]{2,1,0:T(8,128)}, u32[]{:S(2)}, u32[]{:S(2)}) collective-permute-start(f32[2,512,128]{2,1,0:T(8,128)} %pad_maximum_fusion.1), channel_id=1, source_target_pairs={{0,1},{1,2},{2,3},{3,4},{4,5},{5,6},{6,7},{7,8},{8,9},{9,10},{10,1... | collective-permute-start | bytes 1572872 | tf_op jit(solution)/shard_map/ppermute | solution.py:16
  114.2 7.4 %slice-start.4 = ((s8[8388608]{0:T(1024)(128)(4,1)}), s8[4194304]{0:T(1024)(128)(4,1)S(1)}, s32[]{:S(2)}) async-start(s8[8388608]{0:T(1024)(128)(4,1)} %bitcast.197), calls=%async_computation.10 | async-start | bytes 8388608
  117.9 1.9 copy-start.1
  117.9 3.7 %slice-start.5 = ((s8[8388608]{0:T(1024)(128)(4,1)}), s8[4194304]{0:T(1024)(128)(4,1)S(1)}, s32[]{:S(2)}) async-start(s8[8388608]{0:T(1024)(128)(4,1)} %bitcast.197), calls=%async_computation.11 | async-start | bytes 8388608
  121.6 1.0 copy-start.2
  129.3 14.4 %collective-permute-start.2 = (f32[2,512,128]{2,1,0:T(8,128)}, f32[2,512,128]{2,1,0:T(8,128)}, u32[]{:S(2)}, u32[]{:S(2)}) collective-permute-start(f32[2,512,128]{2,1,0:T(8,128)} %pad_maximum_fusion.2), channel_id=1, source_target_pairs={{0,1},{1,2},{2,3},{3,4},{4,5},{5,6},{6,7},{7,8},{8,9},{9,10},{10,1... | collective-permute-start | bytes 1572872 | tf_op jit(solution)/shard_map/ppermute | solution.py:16
  144.3 7.5 %slice-start.6 = ((s8[8388608]{0:T(1024)(128)(4,1)}), s8[4194304]{0:T(1024)(128)(4,1)S(1)}, s32[]{:S(2)}) async-start(s8[8388608]{0:T(1024)(128)(4,1)} %bitcast.199), calls=%async_computation.12 | async-start | bytes 8388608
  148.0 3.7 %slice-start.7 = ((s8[8388608]{0:T(1024)(128)(4,1)}), s8[4194304]{0:T(1024)(128)(4,1)S(1)}, s32[]{:S(2)}) async-start(s8[8388608]{0:T(1024)(128)(4,1)} %bitcast.199), calls=%async_computation.13 | async-start | bytes 8388608
  150.0 3.3 %copy-start.4 = (f32[512,128]{1,0:T(8,128)}, f32[512,128]{1,0:T(8,128)S(1)}, u32[]{:S(2)}) copy-start(f32[512,128]{1,0:T(8,128)S(1)} %get-tuple-element.80) | copy-start | bytes 786436
  157.3 1.6 copy-start.3
  161.0 89.7 %reduce-scatter.3.cloned.1.call-start = ((), (), s32[]{:S(2)}) async-start(), calls=%async_computation.4 | async-start | bytes 2621440 | tf_op jit(solution)/shard_map/reduce_scatter | solution.py:117
Sparse Core Ops, SparseCore 0:
  9.6 40.5 all-gather.1
  161.1 31.7 reduce-scatter.4
  196.1 37.6 reduce-scatter.2
